TPU v7x, 256 devices: a whole 4x4x8 slice. The times are simulated.
256 devices in a mesh: dp: 16 (over z, core), tensor: 16 (over y, x).
Axes of the slice: x: 4, y: 4, z: 8, core: 2. Of those that a mesh axis runs over, the one named last changes fastest.
Arguments:
- tokens: bfloat16 [2048, 8192], P(('dp', 'tensor')), may hold values from -6 to 6
- hidden_grad: bfloat16 [2048, 14336], P('dp', 'tensor'), may hold values from -1.5 to 1.5
- gate_tiles: bfloat16 [16, 208, 128, 128], P('tensor', 'dp'), may hold values from -0.125 to 0.125
- up_tiles: bfloat16 [16, 208, 128, 128], P('tensor', 'dp'), may hold values from -0.125 to 0.125
- tile_rows: int32 [2, 112, 16], P(None, 'tensor'), may hold values from 0 to 63, all different within a row
- tile_owner: int32 [2, 112, 16], P(None, 'tensor'), may hold values from 0 to 15, as said below
Outputs:
- hidden: bfloat16 [2048, 14336], P('dp', 'tensor')
- token_grad: bfloat16 [2048, 8192], P(('dp', 'tensor'))
- gate_grad: bfloat16 [16, 208, 128, 128], P('tensor', 'dp')
- up_grad: bfloat16 [16, 208, 128, 128], P('tensor', 'dp')
Inputs may be any that keep to these rules, and one draw needn't show every extreme that they name: Each row tile_rows[m, f, :] names 16 different row blocks. For each m and t, among the 112 entries tile_owner[m, t * 7 .. (t + 1) * 7 - 1, :] no owner appears more than 13 times, and some owner appears exactly 13 times.
All inputs are finite; a program needn't handle non-finite values.
Results may differ from a plain program's by a relative error of at most 0.018.
Values may be sent and summed in bfloat16 or wider, within the bound.
No kernel may reach another device: no remote copies, remote signals or barrier semaphores. Data moves between devices by JAX's collectives and lax.ppermute only.
A program may use at most 128 MiB of HBM per device.

v0:
```python
import jax
import jax.numpy as jnp
from jax import lax
from jax.sharding import PartitionSpec as P


def slot_index(owner_ids, capacity):
    tile_total = owner_ids.shape[0]
    tile_order = jnp.arange(tile_total, dtype=jnp.int32)
    same_owner = (owner_ids[:, None] == owner_ids[None, :]) & (
        tile_order[None, :] < tile_order[:, None]
    )
    tile_ranks = jnp.sum(same_owner.astype(jnp.int32), axis=1)
    return owner_ids * capacity + tile_ranks


def body(tokens, hidden_grad, gate_tiles, up_tiles, tile_rows, tile_owner):
    tile_size = gate_tiles.shape[2]
    capacity = gate_tiles.shape[1]
    owner_count = lax.axis_size("dp")
    slot_total = capacity * owner_count
    gathered_tok = lax.all_gather(tokens, "tensor", axis=0, tiled=True)
    tok_count, model_width = gathered_tok.shape
    row_blocks = model_width // tile_size
    tok_blocks = gathered_tok.reshape(tok_count, row_blocks, tile_size)
    group_blocks = tile_rows.shape[1]
    per_block = tile_rows.shape[2]
    tile_count = group_blocks * per_block
    block_ids = jnp.arange(tile_count, dtype=jnp.int32) // per_block
    row_flat = tile_rows.reshape(2, tile_count)
    slot_stack = jnp.stack(
        [
            slot_index(tile_owner[0].reshape(-1), capacity),
            slot_index(tile_owner[1].reshape(-1), capacity),
        ],
        axis=0,
    )
    slot_grid = jnp.arange(slot_total, dtype=jnp.int32)
    slot_match = (slot_stack[:, None, :] == slot_grid[None, :, None]).astype(jnp.int32)
    slot_live = jnp.sum(slot_match, axis=2)
    slot_row = jnp.sum(slot_match * row_flat[:, None, :], axis=2)
    slot_block = jnp.sum(slot_match * block_ids[None, None, :], axis=2)
    slot_target = jnp.where(slot_live == 1, slot_block, group_blocks)
    local_gate = gate_tiles[0]
    local_up = up_tiles[0]
    gate_store, up_store = (
        lax.all_gather(local_gate, "dp", axis=0, tiled=True),
        lax.all_gather(local_up, "dp", axis=0, tiled=True),
    )
    gate_panel = jnp.take(gate_store, slot_stack[0], axis=0).reshape(
        group_blocks, per_block, tile_size, tile_size
    )
    up_panel = jnp.take(up_store, slot_stack[1], axis=0).reshape(
        group_blocks, per_block, tile_size, tile_size
    )
    picked = jnp.take(tok_blocks, row_flat.reshape(-1), axis=1).reshape(
        tok_count, 2, group_blocks, per_block, tile_size
    )
    gate_pre = jnp.einsum(
        "nfkr,fkrc->nfc", picked[:, 0], gate_panel, preferred_element_type=jnp.float32
    ).reshape(tok_count, group_blocks * tile_size)
    up_pre = jnp.einsum(
        "nfkr,fkrc->nfc", picked[:, 1], up_panel, preferred_element_type=jnp.float32
    ).reshape(tok_count, group_blocks * tile_size)
    hidden = (jax.nn.silu(gate_pre) * up_pre).astype(jnp.bfloat16)
    gate_sig = jax.nn.sigmoid(gate_pre)
    delta_full = hidden_grad.astype(jnp.float32)
    gate_delta = (delta_full * up_pre * gate_sig * (1.0 + gate_pre * (1.0 - gate_sig))).astype(
        jnp.bfloat16
    )
    up_delta = (delta_full * gate_pre * gate_sig).astype(jnp.bfloat16)
    delta_stack = jnp.stack(
        [
            gate_delta.reshape(tok_count, group_blocks, tile_size),
            up_delta.reshape(tok_count, group_blocks, tile_size),
        ],
        axis=1,
    )
    panel_stack = jnp.stack([gate_panel, up_panel], axis=0)
    back_rows = jnp.einsum(
        "nmfc,mfkrc->mfknr", delta_stack, panel_stack, preferred_element_type=jnp.float32
    )
    back_flat = back_rows.reshape(2 * tile_count, tok_count, tile_size)
    row_sums = jax.ops.segment_sum(back_flat, row_flat.reshape(-1), num_segments=row_blocks)
    token_part = row_sums.transpose(1, 0, 2).reshape(tok_count, model_width)
    token_grad = lax.psum_scatter(
        token_part.astype(jnp.bfloat16), "tensor", scatter_dimension=0, tiled=True
    )
    zero_block = jnp.zeros((tok_count, 2, 1, tile_size), jnp.bfloat16)
    delta_padded = jnp.concatenate([delta_stack, zero_block], axis=2).reshape(
        tok_count, 2 * (group_blocks + 1), tile_size
    )
    matrix_base = jnp.arange(2, dtype=jnp.int32) * (group_blocks + 1)
    target_part = slot_target + matrix_base[:, None]
    chosen = jnp.take(tok_blocks, slot_row.reshape(-1), axis=1).reshape(
        tok_count, 2, capacity * lax.axis_size("dp"), tile_size
    )
    delta_part = jnp.take(delta_padded, target_part.reshape(-1), axis=1).reshape(
        tok_count, 2, capacity * lax.axis_size("dp"), tile_size
    )
    tile_sums = lax.psum_scatter(
        jnp.einsum(
            "nmsr,nmsc->smrc", chosen, delta_part, preferred_element_type=jnp.float32
        ).astype(jnp.bfloat16),
        "dp",
        scatter_dimension=0,
        tiled=True,
    ).astype(jnp.float32)
    gate_grad = tile_sums[:, 0].astype(jnp.bfloat16)[None]
    up_grad = tile_sums[:, 1].astype(jnp.bfloat16)[None]
    return (hidden, token_grad, gate_grad, up_grad)


def solution(mesh):
    placed = (
        P(("dp", "tensor"), None),
        P("dp", "tensor"),
        P("tensor", "dp", None, None),
        P("tensor", "dp", None, None),
        P(None, "tensor", None),
        P(None, "tensor", None),
    )
    return jax.shard_map(
        body,
        mesh=mesh,
        in_specs=placed,
        out_specs=(
            P("dp", "tensor"),
            P(("dp", "tensor"), None),
            P("tensor", "dp", None, None),
            P("tensor", "dp", None, None),
        ),
        check_vma=False,
    )
```

profile of v0, /device:TPU:2, one launch (start us, length us, event | category | flops | bytes accessed | tf_op | source)
XLA Modules:
  0.0 453.2 jit_solution(11754717820026690466)
XLA Ops:
  7.2 0.7 all-gather.6.cloned.1.call-update
  7.9 0.7 all-gather.10.cloned.1.call-update
  8.7 0.7 all-gather.8.cloned.1.call-update
  9.4 0.7 copy.79
  10.4 0.7 compare_and_fusion
  11.1 0.8 multiply_reduce_fusion.1
  12.2 0.2 convert_reduce_fusion.1
  12.4 0.2 convert_reduce_fusion.2
  12.6 0.3 select_reduce_fusion.1
  12.9 0.1 reshape.263
  13.2 1.1 copy.85
  14.4 48.5 %all-gather.6.cloned.1.call-done = bf16[128,8192]{1,0:T(8,128)(2,1)} async-done(((bf16[8,8192]{1,0:T(8,128)(2,1)}), bf16[128,8192]{1,0:T(8,128)(2,1)}) %all-gather.6.cloned.1.call-update) | async-done | bytes 2097168 | tf_op jit(solution)/shard_map/all_gather | solution.py:22
  63.0 4.1 copy.78
  67.1 3.2 copy.80
  70.3 8.3 %gather_fusion = bf16[224,128,128]{2,1,0:T(8,128)(2,1)} fusion(bf16[128,64,128]{2,0,1:T(8,128)(2,1)S(1)} %copy.80, s32[1024]{0:T(1024)S(1)} %pad_clamp_fusion.3), kind=kCustom, calls=%fused_computation.2 | custom fusion | bytes 14680960 | tf_op jit(solution)/shard_map/jit(_take)/gather | solution.py:56
  78.6 12.8 %gather_fusion.1 = bf16[416,128,128]{2,1,0:T(8,128)(2,1)} fusion(bf16[128,64,128]{2,0,1:T(8,128)(2,1)S(1)} %copy.80, s32[1024]{0:T(1024)S(1)} %pad_clamp_fusion.1), kind=kCustom, calls=%fused_computation.3 | custom fusion | bytes 27264640 | tf_op jit(solution)/shard_map/jit(_take)/gather | solution.py:95
  91.5 12.9 %copy.92 = bf16[128,416,128]{2,1,0:T(8,128)(2,1)} copy(bf16[128,416,128]{2,0,1:T(8,128)(2,1)} %bitcast.94) | data formatting | bytes 27262976 | tf_op jit(solution)/shard_map/jit(_take)/gather | solution.py:95
  104.3 3.7 broadcast_select_fusion.2
  108.0 11.5 %broadcast_select_fusion.1 = bf16[128,2,208,128]{3,2,1,0:T(8,128)(2,1)} fusion(bf16[128,2,208,128]{3,2,1,0:T(8,128)(2,1)} %bitcast.92, pred[2,208]{1,0:T(4,128)(4,1)S(1)} %compare_and_fusion.2), kind=kLoop, calls=%fused_computation.10 | loop fusion | flops 6815744 | bytes 27263392 | tf_op jit(solution)/shard_map/jit(_take)/select_n | solution.py:95
  119.5 5.9 %gather_fusion.4 = bf16[112,128,128]{2,1,0:T(8,128)(2,1)} fusion(bf16[208,128,128]{2,1,0:T(8,128)(2,1)} %bitcast.105, s32[1024]{0:T(1024)S(1)} %pad_clamp_fusion.2), kind=kCustom, calls=%fused_computation.1.clone | custom fusion | bytes 7340480 | tf_op jit(solution)/shard_map/jit(_take)/gather | solution.py:53
  125.4 4.3 broadcast_select_fusion.3
  129.8 32.2 %all-gather.8.cloned.1.call-done = bf16[1,208,128,128]{3,2,0,1:T(8,128)(2,1)} async-done(((bf16[1,13,128,128]{3,2,0,1:T(8,128)(2,1)}), bf16[1,208,128,128]{3,2,0,1:T(8,128)(2,1)}) %all-gather.8.cloned.1.call-update) | async-done | bytes 6815760 | tf_op jit(solution)/shard_map/all_gather | solution.py:47
  161.9 6.0 %gather_fusion.3 = bf16[112,128,128]{2,1,0:T(8,128)(2,1)} fusion(bf16[208,128,128]{2,1,0:T(8,128)(2,1)} %bitcast.106, s32[1024]{0:T(1024)S(1)} %pad_clamp_fusion.4), kind=kCustom, calls=%fused_computation.clone | custom fusion | bytes 7340480 | tf_op jit(solution)/shard_map/jit(_take)/gather | solution.py:50
  167.9 2.6 broadcast_select_fusion.4
  170.5 0.5 copy-done.1
  171.0 5.0 %fusion.12 = f32[7,128,128,1]{2,1,3,0:T(8,128)S(1)} fusion(bf16[7,16,128,128]{3,2,1,0:T(8,128)(2,1)S(1)} %bitcast.98, bf16[128,2,7,16,128]{4,0,3,2,1:T(8,128)(2,1)} %broadcast_select_fusion.2), kind=kOutput, calls=%fused_computation.18 | convolution fusion | flops 469762048 | bytes 7798784 | tf_op jit(solution)/shard_map/nfkr,fkrc->nfc/dot_general | solution.py:62
  176.0 1.3 fusion.13
  177.3 0.3 fusion.16
  177.6 0.2 copy.86
  177.8 0.2 copy.87
  178.0 10.5 %fusion.8 = f32[2,7,16,128,128]{4,3,2,1,0:T(8,128)} fusion(bf16[1,7,16,128,128]{4,3,2,1,0:T(8,128)(2,1)} %bitcast.97, bf16[1,7,16,128,128]{4,3,2,1,0:T(8,128)(2,1)} %bitcast.100, bf16[128,1,7,128]{3,0,2,1:T(8,128)(2,1)S(1)} %copy.87, bf16[128,1,7,128]{3,0,2,1:T(8,128)(2,1)S(1)} %copy.86), kind=kOutput, calls=%fused_computation.12 | convolution fusion | flops 943423488 | bytes 22478848 | tf_op jit(solution)/shard_map/nmfc,mfkrc->mfknr/dot_general | solution.py:80
  188.6 15.2 %copy.88 = f32[224,128,128]{2,1,0:T(8,128)} copy(f32[224,128,128]{1,2,0:T(8,128)} %bitcast.91) | data formatting | bytes 29360128 | tf_op jit(solution)/shard_map/reshape | solution.py:83
  203.7 2.5 broadcast_in_dim.57
  206.2 46.3 %scatter_fusion = f32[64,128,128]{2,1,0:T(8,128)} fusion(f32[64,128,128]{2,1,0:T(8,128)} %broadcast_in_dim.57, s32[224]{0:T(256)S(1)} %reshape.307, f32[224,128,128]{2,1,0:T(8,128)} %copy.88), kind=kCustom, calls=%fused_computation.5 | custom fusion | flops 3670016 | bytes 44041088 | tf_op jit(solution)/shard_map/scatter-add | solution.py:84
  252.5 2.6 convert_bitcast_fusion
  255.0 3.0 copy.89
  258.1 12.8 %gather_fusion.2 = bf16[416,128,128]{2,1,0:T(8,128)(2,1)} fusion(bf16[128,16,128]{2,0,1:T(8,128)(2,1)S(1)} %bitcast.90, s32[1024]{0:T(1024)S(1)} %pad_clamp_fusion), kind=kCustom, calls=%fused_computation.4 | custom fusion | bytes 27264640 | tf_op jit(solution)/shard_map/jit(_take)/gather | solution.py:98
  270.9 13.1 %copy.93 = bf16[128,416,128]{2,1,0:T(8,128)(2,1)S(1)} copy(bf16[128,416,128]{2,0,1:T(8,128)(2,1)} %bitcast.95) | data formatting | bytes 27262976 | tf_op jit(solution)/shard_map/jit(_take)/gather | solution.py:98
  284.1 5.8 %broadcast_select_fusion = bf16[128,2,208,128]{3,2,1,0:T(8,128)(2,1)} fusion(bf16[128,2,208,128]{3,2,1,0:T(8,128)(2,1)S(1)} %bitcast.93, pred[2,208]{1,0:T(4,128)(4,1)S(1)} %get-tuple-element.28), kind=kLoop, calls=%fused_computation.9 | loop fusion | flops 6815744 | bytes 27263392 | tf_op jit(solution)/shard_map/jit(_take)/select_n | solution.py:98
  289.8 37.8 %fusion.3 = bf16[208,2,128,128]{3,2,1,0:T(8,128)(2,1)} fusion(bf16[128,2,208,128]{3,2,1,0:T(8,128)(2,1)} %broadcast_select_fusion, bf16[128,2,208,128]{3,2,1,0:T(8,128)(2,1)} %broadcast_select_fusion.1), kind=kOutput, calls=%fused_computation.11 | convolution fusion | flops 1751646208 | bytes 40894464 | tf_op jit(solution)/shard_map/nmsr,nmsc->smrc/dot_general | solution.py:102
  327.6 0.6 copy-done.3
  328.3 0.6 dynamic-slice
  329.5 0.8 copy.96
  330.4 27.2 %all-reduce.4.cloned.1.call-done = bf16[128,8192]{0,1:T(8,128)(2,1)} async-done(((bf16[128,8192]{0,1:T(8,128)(2,1)}), bf16[128,8192]{0,1:T(8,128)(2,1)}) %all-reduce.4.cloned.1.call-update) | async-done | bytes 2097168
  357.6 2.2 constant_dynamic-slice_fusion
  359.8 1.4 copy.97
  361.2 83.3 %reduce-scatter.3.cloned.1.call-done = bf16[13,2,128,128]{3,2,1,0:T(8,128)(2,1)} async-done(((bf16[208,2,128,128]{3,2,1,0:T(8,128)(2,1)}), bf16[13,2,128,128]{3,2,1,0:T(8,128)(2,1)}) %reduce-scatter.3.cloned.1.call-update) | async-done | bytes 851984 | tf_op jit(solution)/shard_map/reduce_scatter | solution.py:101
  444.5 2.1 slice_bitcast_fusion.4
  (46 shorter events, 1.2 us)
Async XLA Ops:
  7.2 55.8 %all-gather.6.cloned.1.call-start = ((), (), s32[]{:S(2)}) async-start(), calls=%async_computation.1 | async-start | bytes 2228224 | tf_op jit(solution)/shard_map/all_gather | solution.py:22
  7.9 111.6 %all-gather.10.cloned.1.call-start = ((), (), s32[]{:S(2)}) async-start(), calls=%async_computation.4 | async-start | bytes 7241728 | tf_op jit(solution)/shard_map/all_gather | solution.py:48
  8.6 153.3 %all-gather.8.cloned.1.call-start = ((), (), s32[]{:S(2)}) async-start(), calls=%async_computation.3 | async-start | bytes 7241728 | tf_op jit(solution)/shard_map/all_gather | solution.py:47
  9.4 348.2 %all-reduce.4.cloned.1.call-start = ((), (), s32[]{:S(2)}) async-start(), calls=%async_computation.5 | async-start | bytes 4194304
  91.5 12.9 %copy-start = (bf16[224,128,128]{2,1,0:T(8,128)(2,1)S(1)}, bf16[224,128,128]{2,1,0:T(8,128)(2,1)}, u32[]{:S(2)}) copy-start(bf16[224,128,128]{2,1,0:T(8,128)(2,1)} %gather_fusion) | copy-start | bytes 22020100
  161.9 14.1 %slice-start = ((s8[7340032]{0:T(1024)(128)(4,1)}), s8[3145728]{0:T(1024)(128)(4,1)S(1)}, s32[]{:S(2)}) async-start(s8[7340032]{0:T(1024)(128)(4,1)} %bitcast.103), calls=%async_computation.6 | async-start | bytes 6291456
  167.9 3.1 copy-start.1
  167.9 8.1 %slice-start.1 = ((s8[7340032]{0:T(1024)(128)(4,1)}), s8[4194304]{0:T(1024)(128)(4,1)S(1)}, s32[]{:S(2)}) async-start(s8[7340032]{0:T(1024)(128)(4,1)} %bitcast.103), calls=%async_computation.7 | async-start | bytes 8388608
  170.5 6.8 %copy-start.2 = (bf16[112,128,128]{2,1,0:T(8,128)(2,1)}, bf16[112,128,128]{2,1,0:T(8,128)(2,1)S(1)}, u32[]{:S(2)}) copy-start(bf16[112,128,128]{2,1,0:T(8,128)(2,1)S(1)} %broadcast_select_fusion.4) | copy-start | bytes 11010052
  258.0 186.5 %reduce-scatter.3.cloned.1.call-start = ((), (), s32[]{:S(2)}) async-start(), calls=%async_computation.2 | async-start | bytes 14483456 | tf_op jit(solution)/shard_map/reduce_scatter | solution.py:101
  327.6 0.7 copy-start.3
Sparse Core Ops, SparseCore 0:
  10.4 52.5 all-gather.5
  64.8 48.1 all-gather.9
  114.8 47.0 all-gather.7
  258.1 99.4 all-reduce.3
  360.0 84.4 reduce-scatter.2
where the time goes:
time: 455 us; the launch traced here: 453 us
  waiting for transfers between devices  193 us (42%)
  local copies, waits for them, and re-layouts  111 us (24%)
  other arithmetic  79.4 us (17%)
  matrix products  54.5 us (12%)
  between operations  14.7 us (3%)
    reduce_scatter x1, waiting for transfers between devices, body(): lax.psum_scatter(jnp.einsum('nmsr,nmsc->smrc', chosen, delta_part, prefer...  83.3 us
    all_gather x1, waiting for transfers between devices, body(): gathered_tok = lax.all_gather(tokens, 'tensor', axis=0, tiled=True)  48.5 us
    scatter-add x1, other arithmetic, body(): jax.ops.segment_sum(back_flat, row_flat.reshape(-1), num_segments=row_blo...  46.3 us
    dot_general x1, matrix products, body(): jnp.einsum('nmsr,nmsc->smrc', chosen, delta_part, preferred_element_type=...  37.8 us
    all_gather x1, waiting for transfers between devices, body(): lax.all_gather(local_gate, 'dp', axis=0, tiled=True)  32.2 us
    unnamed x6, waiting for transfers between devices  29.3 us
    gather x2, local copies, waits for them, and re-layouts, body(): jnp.take(delta_padded, target_part.reshape(-1), axis=1)  25.9 us
    gather x2, local copies, waits for them, and re-layouts, body(): jnp.take(tok_blocks, slot_row.reshape(-1), axis=1)  25.7 us
  transfers between devices with their start and end apart: 5, of which 4 were waited for; matrix products, arithmetic and copies ran while one was open for 32% of the time, Pallas kernels for 0%

commit v1 on v0

--- a/solution.py
+++ b/solution.py
@@ -2,6 +2,13 @@
 import jax.numpy as jnp
 from jax import lax
 from jax.sharding import PartitionSpec as P
+
+
+def convert_groups(here_x, along_axis):
+    upper = jnp.concatenate(
+        lax.all_to_all(jnp.stack(lax.psum(1, along_axis) * [here_x]), along_axis, 0, 0), axis=0
+    )
+    return upper
 
 
 def slot_index(owner_ids, capacity):
@@ -44,7 +51,7 @@
     local_gate = gate_tiles[0]
     local_up = up_tiles[0]
     gate_store, up_store = (
-        lax.all_gather(local_gate, "dp", axis=0, tiled=True),
+        convert_groups(local_gate, "dp"),
         lax.all_gather(local_up, "dp", axis=0, tiled=True),
     )
     gate_panel = jnp.take(gate_store, slot_stack[0], axis=0).reshape(

time: 455 us -> 509 us (1.12)
  waiting for transfers between devices: 193 us -> 237 us
  starting transfers between devices: 0.19 us -> 8.9 us
    all_gather x1, waiting for transfers between devices: 0.01 us -> 83.8 us  [body(): lax.all_gather(local_up, 'dp', axis=0, tiled=True)]
    all_gather x1 -> x0, waiting for transfers between devices: 32.2 us -> none  [body(): lax.all_gather(local_gate, 'dp', axis=0, tiled=True)]
    all_gather x1, waiting for transfers between devices: 48.5 us -> 38.2 us  [body(): gathered_tok = lax.all_gather(tokens, 'tensor', axis=0, tiled=True)]
    all_to_all x0 -> x1, starting transfers between devices: none -> 8.75 us  [convert_groups(): lax.all_to_all(jnp.stack(lax.psum(1, along_axis) * [here_x]), along_axis,...]
    another operation x0 -> x1, local copies, waits for them, and re-layouts: none -> 5.57 us  [convert_groups(): jnp.stack(lax.psum(1, along_axis) * [here_x])]
    unnamed x6 -> x5, waiting for transfers between devices: 29.3 us -> 31.3 us
  transfers between devices with their start and end apart: 5 -> 5, of which waited for: 4 -> 4; matrix products, arithmetic and copies ran while one was open for 32% -> 29% of each run, Pallas kernels for 0% -> 0%
where the time goes in v1:
time: 509 us; the launch traced here: 507 us
  waiting for transfers between devices  237 us (47%)
  local copies, waits for them, and re-layouts  115 us (23%)
  other arithmetic  77.9 us (15%)
  matrix products  54.4 us (11%)
  between operations  14.7 us (3%)
  starting transfers between devices  8.9 us (2%)
    all_gather x1, waiting for transfers between devices, body(): lax.all_gather(local_up, 'dp', axis=0, tiled=True)  83.8 us
    reduce_scatter x1, waiting for transfers between devices, body(): lax.psum_scatter(jnp.einsum('nmsr,nmsc->smrc', chosen, delta_part, prefer...  83.3 us
    scatter-add x1, other arithmetic, body(): jax.ops.segment_sum(back_flat, row_flat.reshape(-1), num_segments=row_blo...  46.3 us
    all_gather x1, waiting for transfers between devices, body(): gathered_tok = lax.all_gather(tokens, 'tensor', axis=0, tiled=True)  38.2 us
    dot_general x1, matrix products, body(): jnp.einsum('nmsr,nmsc->smrc', chosen, delta_part, preferred_element_type=...  37.7 us
    unnamed x5, waiting for transfers between devices  31.3 us
    gather x2, local copies, waits for them, and re-layouts, body(): jnp.take(delta_padded, target_part.reshape(-1), axis=1)  25.9 us
    gather x2, local copies, waits for them, and re-layouts, body(): jnp.take(tok_blocks, slot_row.reshape(-1), axis=1)  25.5 us
  transfers between devices with their start and end apart: 5, of which 4 were waited for; matrix products, arithmetic and copies ran while one was open for 29% of the time, Pallas kernels for 0%

profile of v1, /device:TPU:2, one launch (start us, length us, event | category | flops | bytes accessed | tf_op | source)
XLA Modules:
  0.0 507.3 jit_solution(2182706254111732696)
XLA Ops:
  7.2 0.7 all-gather.4.cloned.1.call-update
  7.9 0.7 all-gather.6.cloned.1.call-update
  8.6 5.6 %stack.14 = bf16[16,13,128,128]{3,2,1,0:T(8,128)(2,1)} broadcast(bf16[13,128,128]{2,1,0:T(8,128)(2,1)} %bitcast.109), dimensions={1,2,3} | broadcast | bytes 7241728 | tf_op jit(solution)/shard_map/stack | solution.py:9
  14.2 8.7 %all-to-all-start = ((bf16[16,13,128,128]{3,2,1,0:T(8,128)(2,1)}), bf16[16,13,128,128]{3,2,1,0:T(8,128)(2,1)}, u32[]{:S(2)}, u32[]{:S(2)}) async-start(bf16[16,13,128,128]{3,2,1,0:T(8,128)(2,1)} %stack.14), calls=%async_computation | async-start | bytes 13631488 | tf_op jit(solution)/shard_map/all_to_all | solution.py:9
  23.0 0.1 mul.94
  23.7 0.2 convert_reduce_fusion.1
  23.9 0.2 convert_reduce_fusion.2
  24.1 0.3 select_reduce_fusion.1
  24.4 0.1 reshape.268
  24.6 0.1 add.157
  24.7 0.2 copy.83
  25.0 38.2 %all-gather.4.cloned.1.call-done = bf16[128,8192]{1,0:T(8,128)(2,1)} async-done(((bf16[8,8192]{1,0:T(8,128)(2,1)}), bf16[128,8192]{1,0:T(8,128)(2,1)}) %all-gather.4.cloned.1.call-update) | async-done | bytes 2097168 | tf_op jit(solution)/shard_map/all_gather | solution.py:29
  63.2 4.1 copy.77
  67.3 3.2 copy.79
  70.5 8.3 %gather_fusion = bf16[224,128,128]{2,1,0:T(8,128)(2,1)} fusion(bf16[128,64,128]{2,0,1:T(8,128)(2,1)S(1)} %copy.79, s32[1024]{0:T(1024)S(1)} %pad_clamp_fusion.3), kind=kCustom, calls=%fused_computation.2 | custom fusion | bytes 14680960 | tf_op jit(solution)/shard_map/jit(_take)/gather | solution.py:63
  78.8 12.8 %gather_fusion.1 = bf16[416,128,128]{2,1,0:T(8,128)(2,1)} fusion(bf16[128,64,128]{2,0,1:T(8,128)(2,1)S(1)} %copy.79, s32[1024]{0:T(1024)S(1)} %pad_clamp_fusion.1), kind=kCustom, calls=%fused_computation.3 | custom fusion | bytes 27264640 | tf_op jit(solution)/shard_map/jit(_take)/gather | solution.py:102
  91.6 12.7 %copy.90 = bf16[128,416,128]{2,1,0:T(8,128)(2,1)} copy(bf16[128,416,128]{2,0,1:T(8,128)(2,1)} %bitcast.95) | data formatting | bytes 27262976 | tf_op jit(solution)/shard_map/jit(_take)/gather | solution.py:102
  104.3 3.6 broadcast_select_fusion.2
  108.0 11.5 %broadcast_select_fusion.1 = bf16[128,2,208,128]{3,2,1,0:T(8,128)(2,1)} fusion(bf16[128,2,208,128]{3,2,1,0:T(8,128)(2,1)} %bitcast.93, pred[2,208]{1,0:T(4,128)(4,1)S(1)} %compare_and_fusion.2), kind=kLoop, calls=%fused_computation.10 | loop fusion | flops 6815744 | bytes 27263392 | tf_op jit(solution)/shard_map/jit(_take)/select_n | solution.py:102
  119.5 83.8 %all-gather.6.cloned.1.call-done = bf16[1,208,128,128]{3,2,0,1:T(8,128)(2,1)} async-done(((bf16[1,13,128,128]{3,2,0,1:T(8,128)(2,1)}), bf16[1,208,128,128]{3,2,0,1:T(8,128)(2,1)}) %all-gather.6.cloned.1.call-update) | async-done | bytes 6815760 | tf_op jit(solution)/shard_map/all_gather | solution.py:55
  203.3 5.8 %gather_fusion.4 = bf16[112,128,128]{2,1,0:T(8,128)(2,1)} fusion(bf16[208,128,128]{2,1,0:T(8,128)(2,1)} %bitcast.106, s32[1024]{0:T(1024)S(1)} %pad_clamp_fusion.2), kind=kCustom, calls=%fused_computation.1.clone | custom fusion | bytes 7340480 | tf_op jit(solution)/shard_map/jit(_take)/gather | solution.py:60
  209.1 4.3 broadcast_select_fusion.3
  213.4 6.0 %gather_fusion.3 = bf16[112,128,128]{2,1,0:T(8,128)(2,1)} fusion(bf16[208,128,128]{2,1,0:T(8,128)(2,1)} %bitcast.1, s32[1024]{0:T(1024)S(1)} %pad_clamp_fusion.4), kind=kCustom, calls=%fused_computation.clone | custom fusion | bytes 7340480 | tf_op jit(solution)/shard_map/jit(_take)/gather | solution.py:57
  219.4 2.6 broadcast_select_fusion.4
  222.0 0.5 copy-done.1
  222.5 5.0 fusion.12
  227.5 1.3 fusion.13
  228.8 0.3 fusion.16
  229.1 0.2 copy.84
  229.3 0.2 copy.85
  229.5 10.5 %fusion.8 = f32[2,7,16,128,128]{4,3,2,1,0:T(8,128)} fusion(bf16[1,7,16,128,128]{4,3,2,1,0:T(8,128)(2,1)} %bitcast.98, bf16[1,7,16,128,128]{4,3,2,1,0:T(8,128)(2,1)} %bitcast.101, bf16[128,1,7,128]{3,0,2,1:T(8,128)(2,1)S(1)} %copy.85, bf16[128,1,7,128]{3,0,2,1:T(8,128)(2,1)S(1)} %copy.84), kind=kOutput, calls=%fused_computation.12 | convolution fusion | flops 943423488 | bytes 22478848 | tf_op jit(solution)/shard_map/nmfc,mfkrc->mfknr/dot_general | solution.py:87
  240.0 15.2 %copy.86 = f32[224,128,128]{2,1,0:T(8,128)} copy(f32[224,128,128]{1,2,0:T(8,128)} %bitcast.92) | data formatting | bytes 29360128 | tf_op jit(solution)/shard_map/reshape | solution.py:90
  255.2 2.5 broadcast_in_dim.57
  257.6 46.3 %scatter_fusion = f32[64,128,128]{2,1,0:T(8,128)} fusion(f32[64,128,128]{2,1,0:T(8,128)} %broadcast_in_dim.57, s32[224]{0:T(256)S(1)} %reshape.312, f32[224,128,128]{2,1,0:T(8,128)} %copy.86), kind=kCustom, calls=%fused_computation.5 | custom fusion | flops 3670016 | bytes 44041088 | tf_op jit(solution)/shard_map/scatter-add | solution.py:91
  304.0 2.6 convert_bitcast_fusion
  306.5 3.0 copy.87
  309.6 12.8 %gather_fusion.2 = bf16[416,128,128]{2,1,0:T(8,128)(2,1)} fusion(bf16[128,16,128]{2,0,1:T(8,128)(2,1)S(1)} %bitcast.91, s32[1024]{0:T(1024)S(1)} %pad_clamp_fusion), kind=kCustom, calls=%fused_computation.4 | custom fusion | bytes 27264640 | tf_op jit(solution)/shard_map/jit(_take)/gather | solution.py:105
  322.4 13.1 %copy.91 = bf16[128,416,128]{2,1,0:T(8,128)(2,1)S(1)} copy(bf16[128,416,128]{2,0,1:T(8,128)(2,1)} %bitcast.96) | data formatting | bytes 27262976 | tf_op jit(solution)/shard_map/jit(_take)/gather | solution.py:105
  335.5 5.8 %broadcast_select_fusion = bf16[128,2,208,128]{3,2,1,0:T(8,128)(2,1)} fusion(bf16[128,2,208,128]{3,2,1,0:T(8,128)(2,1)S(1)} %bitcast.94, pred[2,208]{1,0:T(4,128)(4,1)S(1)} %get-tuple-element.28), kind=kLoop, calls=%fused_computation.9 | loop fusion | flops 6815744 | bytes 27263392 | tf_op jit(solution)/shard_map/jit(_take)/select_n | solution.py:105
  341.3 37.7 %fusion.3 = bf16[208,2,128,128]{3,2,1,0:T(8,128)(2,1)} fusion(bf16[128,2,208,128]{3,2,1,0:T(8,128)(2,1)} %broadcast_select_fusion, bf16[128,2,208,128]{3,2,1,0:T(8,128)(2,1)} %broadcast_select_fusion.1), kind=kOutput, calls=%fused_computation.11 | convolution fusion | flops 1751646208 | bytes 40894464 | tf_op jit(solution)/shard_map/nmsr,nmsc->smrc/dot_general | solution.py:109
  379.0 0.6 copy-done.6
  379.7 0.6 dynamic-slice
  380.9 0.8 copy.94
  381.8 29.9 %all-reduce.4.cloned.1.call-done = bf16[128,8192]{0,1:T(8,128)(2,1)} async-done(((bf16[128,8192]{0,1:T(8,128)(2,1)}), bf16[128,8192]{0,1:T(8,128)(2,1)}) %all-reduce.4.cloned.1.call-update) | async-done | bytes 2097168
  411.7 2.2 constant_dynamic-slice_fusion
  413.9 1.4 copy.95
  415.3 83.3 %reduce-scatter.3.cloned.1.call-done = bf16[13,2,128,128]{3,2,1,0:T(8,128)(2,1)} async-done(((bf16[208,2,128,128]{3,2,1,0:T(8,128)(2,1)}), bf16[13,2,128,128]{3,2,1,0:T(8,128)(2,1)}) %reduce-scatter.3.cloned.1.call-update) | async-done | bytes 851984 | tf_op jit(solution)/shard_map/reduce_scatter | solution.py:108
  498.6 2.1 slice_bitcast_fusion.4
  (52 shorter events, 1.0 us)
Async XLA Ops:
  7.2 56.0 %all-gather.4.cloned.1.call-start = ((), (), s32[]{:S(2)}) async-start(), calls=%async_computation.2 | async-start | bytes 2228224 | tf_op jit(solution)/shard_map/all_gather | solution.py:29
  7.9 195.4 %all-gather.6.cloned.1.call-start = ((), (), s32[]{:S(2)}) async-start(), calls=%async_computation.4 | async-start | bytes 7241728 | tf_op jit(solution)/shard_map/all_gather | solution.py:55
  14.2 8.8 %copy-start.4 = (s32[2,7,16]{2,0,1:T(2,128)S(1)}, s32[2,7,16]{2,0,1:T(2,128)}, u32[]{:S(2)}) copy-start(s32[2,7,16]{2,0,1:T(2,128)} %param.12) | copy-start | bytes 2692
  14.2 9.1 %copy-start.5 = (s32[2,7,16]{2,0,1:T(2,128)S(1)}, s32[2,7,16]{2,0,1:T(2,128)}, u32[]{:S(2)}) copy-start(s32[2,7,16]{2,0,1:T(2,128)} %param.13) | copy-start | bytes 2692
  14.2 10.4 %copy-start.3 = (bf16[128,896]{1,0:T(8,128)(2,1)S(1)}, bf16[128,896]{1,0:T(8,128)(2,1)}, u32[]{:S(2)}) copy-start(bf16[128,896]{1,0:T(8,128)(2,1)} %param.9) | copy-start | bytes 688132
  14.2 199.2 %all-to-all-start = ((bf16[16,13,128,128]{3,2,1,0:T(8,128)(2,1)}), bf16[16,13,128,128]{3,2,1,0:T(8,128)(2,1)}, u32[]{:S(2)}, u32[]{:S(2)}) async-start(bf16[16,13,128,128]{3,2,1,0:T(8,128)(2,1)} %stack.14), calls=%async_computation | async-start | bytes 13631488 | tf_op jit(solution)/shard_map/all_to_all | solution.py:9
  23.0 388.7 %all-reduce.4.cloned.1.call-start = ((), (), s32[]{:S(2)}) async-start(), calls=%async_computation.5 | async-start | bytes 4194304
  91.6 12.7 %copy-start = (bf16[224,128,128]{2,1,0:T(8,128)(2,1)S(1)}, bf16[224,128,128]{2,1,0:T(8,128)(2,1)}, u32[]{:S(2)}) copy-start(bf16[224,128,128]{2,1,0:T(8,128)(2,1)} %gather_fusion) | copy-start | bytes 22020100
  213.4 14.1 %slice-start = ((s8[7340032]{0:T(1024)(128)(4,1)}), s8[3145728]{0:T(1024)(128)(4,1)S(1)}, s32[]{:S(2)}) async-start(s8[7340032]{0:T(1024)(128)(4,1)} %bitcast.104), calls=%async_computation.6 | async-start | bytes 6291456
  219.4 3.1 copy-start.1
  219.4 8.1 %slice-start.1 = ((s8[7340032]{0:T(1024)(128)(4,1)}), s8[4194304]{0:T(1024)(128)(4,1)S(1)}, s32[]{:S(2)}) async-start(s8[7340032]{0:T(1024)(128)(4,1)} %bitcast.104), calls=%async_computation.7 | async-start | bytes 8388608
  222.0 6.8 %copy-start.2 = (bf16[112,128,128]{2,1,0:T(8,128)(2,1)}, bf16[112,128,128]{2,1,0:T(8,128)(2,1)S(1)}, u32[]{:S(2)}) copy-start(bf16[112,128,128]{2,1,0:T(8,128)(2,1)S(1)} %broadcast_select_fusion.4) | copy-start | bytes 11010052
  309.5 189.1 %reduce-scatter.3.cloned.1.call-start = ((), (), s32[]{:S(2)}) async-start(), calls=%async_computation.3 | async-start | bytes 14483456 | tf_op jit(solution)/shard_map/reduce_scatter | solution.py:108
  379.0 0.7 copy-start.6
Sparse Core Ops, SparseCore 0:
  10.4 52.7 all-gather.3
  65.0 138.2 all-gather.5
  309.6 101.9 all-reduce.3
  414.1 84.4 reduce-scatter.2
